TPU v7x, 32 devices: a whole 2x2x4 slice. The times are simulated.
32 devices in a mesh: shot: 4 (over y, core), mesh: 8 (over z, x).
Axes of the slice: x: 2, y: 2, z: 4, core: 2. Of those that a mesh axis runs over, the one named last changes fastest.
Arguments:
- adjoint_state: float32 [4, 13, 35, 1024], P('shot', None, None, 'mesh'), may hold values from -6 to 6
- forward_states: float32 [4, 2, 13, 35, 1024], P('shot', None, None, None, 'mesh'), may hold values from -6 to 6
- material: float32 [6, 35, 1024], P(None, None, 'mesh'), may hold values from 0.5 to 2
- coupling: float32 [3, 6, 13, 13], replicated, may hold values from -0.375 to 0.375
- metric: float32 [3, 3, 1024], P(None, None, 'mesh'), may hold values from -4 to 4
- face_normals: float32 [3, 4, 1024], P(None, None, 'mesh'), may hold values from -4 to 4
- face_scale: float32 [4, 1024], P(None, 'mesh'), may hold values from 1 to 3
- face_neighbours: int32 [4, 1024], P(None, 'mesh'), may hold values from 0 to 639, as said below
- face_orientation: int32 [4, 1024], P(None, 'mesh'), may hold values from 0 to 5
- send_faces: int32 [1024], P('mesh'), may hold values from 0 to 511, as said below
- history_steps: float32 [5, 6, 35, 1024], P(None, None, None, 'mesh')
- history_changes: float32 [5, 6, 35, 1024], P(None, None, None, 'mesh'), as said below
Outputs:
- adjoint_final: float32 [4, 13, 35, 1024], P('shot', None, None, 'mesh')
- direction: float32 [6, 35, 1024], P(None, None, ('mesh', 'shot'))
Inputs may be any that keep to these rules, and one draw needn't show every extreme that they name: `face_neighbours`: local faces of a partition are numbered x * 128 + e. Each face either forms a pair with another local face (each names the other) or reads exactly one of the 128 ghost slots, and every ghost slot is read by exactly one face; on every partition the face that reads slot 512 + j is send_faces[j] and the face that reads slot 576 + j is send_faces[64 + j]. `send_faces`: the 128 entries of one partition are distinct local face numbers. `history_changes`: for every stored pair, s_i . y_i is positive.
All inputs are finite; a program needn't handle non-finite values.
Results may differ from a plain program's by a relative error of at most 0.0003.
Values sent between devices are 32-bit elements; how exact they have to be, the bound alone decides.
No kernel may reach another device: no remote copies, remote signals or barrier semaphores. Data moves between devices by JAX's collectives and lax.ppermute only.
A program may use at most 64 MiB of HBM per device.

v0:
```python
import math
import jax
import jax.numpy as jnp
import numpy as np
from jax import lax
from jax.sharding import PartitionSpec as P

HIGH = lax.Precision.HIGHEST
STEP_SIZE = 0.02


def padded(x, sides, width):
    for axis, dim in sides:
        devices, length = (lax.axis_size(axis), x.shape[dim])
        up = [(i, (i + 1) % devices) for i in range(devices - 1)]
        down = [(j, i) for i, j in up]
        last = lax.slice_in_dim(x, length - width, length, axis=dim)
        first = lax.slice_in_dim(x, 0, width, axis=dim)
        before = lax.ppermute(last, axis, up)
        after = lax.ppermute(first, axis, down)
        x = jnp.concatenate([before, x, after], axis=dim)
    return x


def invert_matrix(matrix):
    order_count = matrix.shape[0]
    working = np.concatenate([matrix * 1.0, np.eye(order_count)], axis=1)
    for column in range(order_count):
        pivot_row = column + int(np.argmax(np.abs(working[column:, column])))
        working[[column, pivot_row]] = working[[pivot_row, column]]
        working[column] = working[column] / working[column, column]
        for target in range(order_count):
            if target != column:
                working[target] = working[target] - working[target, column] * working[column]
    return working[:, order_count:]


def basis_tables():
    points = [
        (across, along, upward)
        for upward in range(5)
        for along in range(5 - upward)
        for across in range(5 - upward - along)
    ]
    exponents = np.array(points) * 1.0
    coords = exponents / 4.0
    vander = np.prod(coords[:, None, :] ** exponents[None, :, :], axis=2)
    inverse = invert_matrix(vander)
    derivs = []
    for direction_axis in range(3):
        lowered = np.maximum(exponents - np.eye(3)[direction_axis], 0.0)
        slopes = exponents[None, :, direction_axis] * np.prod(
            coords[:, None, :] ** lowered[None, :, :], axis=2
        )
        derivs.append(slopes @ inverse)
    moments = np.array(
        [
            [
                math.factorial(first[0] + second[0])
                * math.factorial(first[1] + second[1])
                * math.factorial(first[2] + second[2])
                / math.factorial(sum(first) + sum(second) + 3)
                for second in points
            ]
            for first in points
        ]
    )
    mass_matrix = inverse.T @ moments @ inverse
    lattice = [(across, along) for along in range(5) for across in range(5 - along)]
    lattice_powers = np.array(lattice) * 1.0
    face_vander = np.prod((lattice_powers / 4.0)[:, None, :] ** lattice_powers[None, :, :], axis=2)
    face_inverse = invert_matrix(face_vander)
    face_moments = np.array(
        [
            [
                math.factorial(first[0] + second[0])
                * math.factorial(first[1] + second[1])
                / math.factorial(sum(first) + sum(second) + 2)
                for second in lattice
            ]
            for first in lattice
        ]
    )
    face_mass = face_inverse.T @ face_moments @ face_inverse
    numbers = {point: number for number, point in enumerate(points)}
    face_points = [
        [(across, along, 0) for across, along in lattice],
        [(across, 0, along) for across, along in lattice],
        [(0, across, along) for across, along in lattice],
        [(across, along, 4 - across - along) for across, along in lattice],
    ]
    face_nodes = np.array(
        [[numbers[point] for point in listing] for listing in face_points], np.int32
    )
    mass_inverse = invert_matrix(mass_matrix)
    lift_tables = []
    for face_number in range(4):
        selector = np.eye(35)[face_nodes[face_number]]
        lift_tables.append(mass_inverse @ selector.T @ face_mass)
    orderings = [(0, 1, 2), (1, 2, 0), (2, 0, 1), (1, 0, 2), (0, 2, 1), (2, 1, 0)]
    lattice_numbers = {point: number for number, point in enumerate(lattice)}
    triples = [(across, along, 4 - across - along) for across, along in lattice]
    turn_nodes = np.array(
        [
            [lattice_numbers[triple[ordering[0]], triple[ordering[1]]] for triple in triples]
            for ordering in orderings
        ],
        np.int32,
    )
    return (
        jnp.asarray(np.stack(derivs), jnp.float32),
        jnp.asarray(np.stack(lift_tables), jnp.float32),
        face_nodes,
        turn_nodes,
    )


def spatial_of(field, metric, derivs):
    reference_grads = jnp.einsum("rab,fbe->rfae", derivs, field, precision=HIGH)
    rows = []
    for direction_axis in range(3):
        total = metric[0, direction_axis] * reference_grads[0]
        total = total + metric[1, direction_axis] * reference_grads[1]
        total = total + metric[2, direction_axis] * reference_grads[2]
        rows.append(total)
    return jnp.stack(rows)


def volume_term(adjoint, material, coupling, metric, derivs):
    spatial = spatial_of(adjoint, metric, derivs)
    mixing = jnp.einsum("dpfg,dfae->pgae", coupling, spatial, precision=HIGH)
    return jnp.sum(material[:, None] * mixing, axis=0)


def kernel_term(adjoint, forward, coupling, metric, derivs):
    spatial = spatial_of(forward, metric, derivs)
    mixing = jnp.einsum("dpfg,dgae->pfae", coupling, spatial, precision=HIGH)
    return jnp.sum(mixing * adjoint[None], axis=1)


def surface_term(jump_trace, face_material, face_normals, face_scale, coupling, lift_tables):
    weighted = face_normals[:, None, None] * jump_trace[None]
    mixing = jnp.einsum("dpfg,dfnxe->pgnxe", coupling, weighted, precision=HIGH)
    face_flux = 0.5 * jnp.sum(face_material[:, None] * mixing, axis=0) + 0.5 * jump_trace
    return jnp.einsum(
        "xan,fnxe->fae", lift_tables, face_flux * face_scale[None, None], precision=HIGH
    )


def search_direction(total_grad, step_rows, change_rows, combine_sums):
    pairs = step_rows.shape[0]
    summed = combine_sums(
        jnp.concatenate(
            [
                jnp.sum(step_rows * change_rows, axis=(1, 2, 3)),
                jnp.sum(change_rows[pairs - 1] * change_rows[pairs - 1])[None],
            ]
        )
    )
    curvature = summed[:pairs]
    alphas = [None] * pairs
    work = total_grad
    for slot in reversed(range(pairs)):
        alphas[slot] = combine_sums(jnp.sum(step_rows[slot] * work)) / curvature[slot]
        work = work - alphas[slot] * change_rows[slot]
    work = curvature[pairs - 1] / summed[pairs] * work
    for slot in range(pairs):
        beta_now = combine_sums(jnp.sum(change_rows[slot] * work)) / curvature[slot]
        work = work + (alphas[slot] - beta_now) * step_rows[slot]
    return -work


def shards(
    adjoint_state,
    forward_states,
    material,
    coupling,
    metric,
    face_normals,
    face_scale,
    face_neighbours,
    face_orientation,
    send_faces,
    history_steps,
    history_changes,
):
    derivs, lift_tables, face_nodes, turn_nodes = basis_tables()
    fields = adjoint_state.shape[1]
    elements = adjoint_state.shape[3]
    node_count = material.shape[1]
    params = material.shape[0]
    face_width = face_nodes.shape[1]
    border = send_faces.shape[0] // 2
    slot_count = 4 * elements + 2 * border
    adjoint = adjoint_state[0]
    face_material = material[:, face_nodes.T, :]
    neighbours = face_neighbours.reshape(-1)
    orient = face_orientation.reshape(-1)
    node_pick = jnp.zeros((face_width, 4 * elements), jnp.int32)
    for option in range(turn_nodes.shape[0]):
        node_pick = (
            node_pick
            + (orient == option).astype(jnp.int32)[None, :]
            * jnp.asarray(turn_nodes[option], jnp.int32)[:, None]
        )
    flat_index = (node_pick * slot_count + neighbours[None, :]).reshape(-1)
    gradient = jnp.zeros((params, node_count, elements), jnp.float32)
    for step_index in range(forward_states.shape[1]):
        inner_trace = adjoint[:, face_nodes.T, :]
        flat_trace = inner_trace.reshape(fields, face_width, 4 * elements)
        sent_traces = flat_trace[:, :, send_faces]
        extended = padded(sent_traces, (("mesh", 2),), border)
        ghosts = jnp.concatenate(
            [flat_trace, extended[:, :, :border], extended[:, :, 3 * border :]], axis=2
        )
        turned = ghosts.reshape(fields, face_width * slot_count)[:, flat_index]
        jump_trace = turned.reshape(fields, face_width, 4, elements) - inner_trace
        change = volume_term(adjoint, material, coupling, metric, derivs) + surface_term(
            jump_trace, face_material, face_normals, face_scale, coupling, lift_tables
        )
        adjoint = adjoint + STEP_SIZE * change
        gradient = gradient + STEP_SIZE * kernel_term(
            adjoint, forward_states[0, step_index], coupling, metric, derivs
        )
    total_grad = lax.psum(gradient, "shot")

    def combine_sums(values):
        return lax.psum(values, "mesh")

    result = search_direction(total_grad, history_steps, history_changes, combine_sums)
    share_width = elements // lax.axis_size("shot")
    result = lax.dynamic_slice_in_dim(result, lax.axis_index("shot") * share_width, share_width, 2)
    return (adjoint[None], result)


def solution(mesh):
    placed = (
        P("shot", None, None, "mesh"),
        P("shot", None, None, None, "mesh"),
        P(None, None, "mesh"),
        P(),
        P(None, None, "mesh"),
        P(None, None, "mesh"),
        P(None, "mesh"),
        P(None, "mesh"),
        P(None, "mesh"),
        P("mesh"),
        P(None, None, None, "mesh"),
        P(None, None, None, "mesh"),
    )
    return jax.shard_map(
        shards,
        mesh=mesh,
        in_specs=placed,
        out_specs=(P("shot", None, None, "mesh"), P(None, None, ("mesh", "shot"))),
        check_vma=False,
    )
```

profile of v0, /device:TPU:0, one launch (start us, length us, event | category | flops | bytes accessed | tf_op | source)
XLA Modules:
  0.0 404.9 jit_solution(5043594300675908869)
XLA Ops:
  9.8 3.6 copy.157
  13.5 3.8 gather_fusion.2
  21.2 6.3 %collective-permute-start = (f32[13,15,64]{1,0,2:T(8,128)}, f32[13,15,64]{1,0,2:T(8,128)}, u32[]{:S(2)}, u32[]{:S(2)}) collective-permute-start(f32[13,15,64]{1,0,2:T(8,128)} %get-tuple-element.22), channel_id=1, source_target_pairs={{0,1},{1,2},{2,3},{3,4},{4,5},{5,6},{6,7},{8,9},{9,10},{10,11},{11... | collective-permute-start | bytes 149768 | tf_op jit(solution)/shard_map/ppermute | solution.py:19
  40.8 7.6 %collective-permute-done = f32[13,15,64]{1,0,2:T(8,128)} collective-permute-done((f32[13,15,64]{1,0,2:T(8,128)}, f32[13,15,64]{1,0,2:T(8,128)}, u32[]{:S(2)}, u32[]{:S(2)}) %collective-permute-start) | collective-permute-done | bytes 49952 | tf_op jit(solution)/shard_map/ppermute | solution.py:19
  53.0 17.3 %gather_fusion.3 = f32[7680,13]{1,0:T(8,128)} fusion(f32[13,9600]{0,1:T(8,128)} %bitcast.349, s32[8192]{0:T(1024)S(1)} %pad_clamp_fusion), kind=kCustom, calls=%fused_computation.3 | custom fusion | bytes 829440 | tf_op jit(solution)/shard_map/gather | solution.py:216
  73.1 3.6 fusion.1
  81.2 3.6 copy.170
  84.8 3.9 gather_fusion.5
  92.2 5.8 %collective-permute-start.2 = (f32[13,15,64]{1,0,2:T(8,128)}, f32[13,15,64]{1,0,2:T(8,128)}, u32[]{:S(2)}, u32[]{:S(2)}) collective-permute-start(f32[13,15,64]{1,0,2:T(8,128)} %get-tuple-element.20), channel_id=1, source_target_pairs={{0,1},{1,2},{2,3},{3,4},{4,5},{5,6},{6,7},{8,9},{9,10},{10,11},{11... | collective-permute-start | bytes 149768 | tf_op jit(solution)/shard_map/ppermute | solution.py:19
  103.0 4.5 %collective-permute-done.3 = f32[13,15,64]{1,0,2:T(8,128)} collective-permute-done((f32[13,15,64]{1,0,2:T(8,128)S(1)}, f32[13,15,64]{1,0,2:T(8,128)}, u32[]{:S(2)}, u32[]{:S(2)}) %collective-permute-start.3) | collective-permute-done | bytes 49952 | tf_op jit(solution)/shard_map/ppermute | solution.py:20
  108.7 10.1 %collective-permute-done.2 = f32[13,15,64]{1,0,2:T(8,128)} collective-permute-done((f32[13,15,64]{1,0,2:T(8,128)}, f32[13,15,64]{1,0,2:T(8,128)}, u32[]{:S(2)}, u32[]{:S(2)}) %collective-permute-start.2) | collective-permute-done | bytes 49952 | tf_op jit(solution)/shard_map/ppermute | solution.py:19
  120.2 3.2 copy.173
  123.5 17.3 %gather_fusion.6 = f32[7680,13]{1,0:T(8,128)} fusion(f32[13,9600]{0,1:T(8,128)} %bitcast.348, s32[8192]{0:T(1024)S(1)} %pad_clamp_fusion), kind=kCustom, calls=%fused_computation.6 | custom fusion | bytes 829440 | tf_op jit(solution)/shard_map/gather | solution.py:216
  150.6 31.2 %all-reduce.3.cloned.1.call-done = f32[6,35,128]{2,0,1:T(8,128)} async-done(((f32[6,35,128]{2,0,1:T(8,128)}), f32[6,35,128]{2,0,1:T(8,128)}) %all-reduce.3.cloned.1.call-update) | async-done | bytes 107536 | tf_op jit(solution)/shard_map/psum | solution.py:225
  183.3 22.0 %all-reduce = (f32[]{:T(128)}, f32[6]{0:T(128)S(1)}) all-reduce(f32[]{:T(128)} %multiply_reduce_fusion.1, f32[6]{0:T(128)S(1)} %pad_maximum_fusion.2), channel_id=1, replica_groups=mesh['shot'=4,'mesh'=8] {'mesh'}, use_global_device_ids=true, to_apply=%region_11.0 | all-reduce | flops 7 | bytes 56 | tf_op jit(solution)/shard_map/psum | solution.py:228
  208.8 17.8 %psum.87 = f32[]{:T(128)} all-reduce(f32[]{:T(128)} %fusion.63), channel_id=1, replica_groups=mesh['shot'=4,'mesh'=8] {'mesh'}, use_global_device_ids=true, to_apply=%region_13.0 | all-reduce | flops 1 | bytes 8 | tf_op jit(solution)/shard_map/psum | solution.py:228
  229.5 19.7 %psum.88 = f32[]{:T(128)} all-reduce(f32[]{:T(128)} %get-tuple-element.18), channel_id=1, replica_groups=mesh['shot'=4,'mesh'=8] {'mesh'}, use_global_device_ids=true, to_apply=%region_15.0 | all-reduce | flops 1 | bytes 8 | tf_op jit(solution)/shard_map/psum | solution.py:228
  251.2 17.8 %psum.89 = f32[]{:T(128)} all-reduce(f32[]{:T(128)} %fusion.47), channel_id=1, replica_groups=mesh['shot'=4,'mesh'=8] {'mesh'}, use_global_device_ids=true, to_apply=%region_17.0 | all-reduce | flops 1 | bytes 8 | tf_op jit(solution)/shard_map/psum | solution.py:228
  271.0 19.7 %psum.90 = f32[]{:T(128)} all-reduce(f32[]{:T(128)} %get-tuple-element.16), channel_id=1, replica_groups=mesh['shot'=4,'mesh'=8] {'mesh'}, use_global_device_ids=true, to_apply=%region_19.0 | all-reduce | flops 1 | bytes 8 | tf_op jit(solution)/shard_map/psum | solution.py:228
  294.1 17.8 %psum.91 = f32[]{:T(128)} all-reduce(f32[]{:T(128)} %fusion.36), channel_id=1, replica_groups=mesh['shot'=4,'mesh'=8] {'mesh'}, use_global_device_ids=true, to_apply=%region_21.0 | all-reduce | flops 1 | bytes 8 | tf_op jit(solution)/shard_map/psum | solution.py:228
  313.9 19.8 %psum.92 = f32[]{:T(128)} all-reduce(f32[]{:T(128)} %fusion.44), channel_id=1, replica_groups=mesh['shot'=4,'mesh'=8] {'mesh'}, use_global_device_ids=true, to_apply=%region_23.0 | all-reduce | flops 1 | bytes 8 | tf_op jit(solution)/shard_map/psum | solution.py:228
  335.7 17.7 %psum.93 = f32[]{:T(128)} all-reduce(f32[]{:T(128)} %get-tuple-element.14), channel_id=1, replica_groups=mesh['shot'=4,'mesh'=8] {'mesh'}, use_global_device_ids=true, to_apply=%region_25.0 | all-reduce | flops 1 | bytes 8 | tf_op jit(solution)/shard_map/psum | solution.py:228
  356.3 19.7 %psum.94 = f32[]{:T(128)} all-reduce(f32[]{:T(128)} %fusion.60), channel_id=1, replica_groups=mesh['shot'=4,'mesh'=8] {'mesh'}, use_global_device_ids=true, to_apply=%region_27.0 | all-reduce | flops 1 | bytes 8 | tf_op jit(solution)/shard_map/psum | solution.py:228
  378.1 17.7 %psum.95 = f32[]{:T(128)} all-reduce(f32[]{:T(128)} %get-tuple-element.12), channel_id=1, replica_groups=mesh['shot'=4,'mesh'=8] {'mesh'}, use_global_device_ids=true, to_apply=%region_29.0 | all-reduce | flops 1 | bytes 8 | tf_op jit(solution)/shard_map/psum | solution.py:228
  (155 shorter events, 63.8 us)
Async XLA Ops:
  7.2 174.6 %all-reduce.3.cloned.1.call-start = ((), (), s32[]{:S(2)}) async-start(), calls=%async_computation | async-start | bytes 286720 | tf_op jit(solution)/shard_map/psum | solution.py:225
  9.8 17.7 %copy-start.2 = (f32[5,6,35,128]{3,2,1,0:T(8,128)S(1)}, f32[5,6,35,128]{3,2,1,0:T(8,128)}, u32[]{:S(2)}) copy-start(f32[5,6,35,128]{3,2,1,0:T(8,128)} %param.37) | copy-start | bytes 1612804
  9.8 17.7 %copy-start.3 = (f32[5,6,35,128]{3,2,1,0:T(8,128)S(1)}, f32[5,6,35,128]{3,2,1,0:T(8,128)}, u32[]{:S(2)}) copy-start(f32[5,6,35,128]{3,2,1,0:T(8,128)} %param.36) | copy-start | bytes 1612804
  13.5 15.6 %copy-start.26 = (s32[4,128]{1,0:T(4,128)S(1)}, s32[4,128]{1,0:T(4,128)}, u32[]{:S(2)}) copy-start(s32[4,128]{1,0:T(4,128)} %param.34) | copy-start | bytes 6148
  17.3 11.8 %copy-start.27 = (s32[4,128]{1,0:T(4,128)S(1)}, s32[4,128]{1,0:T(4,128)}, u32[]{:S(2)}) copy-start(s32[4,128]{1,0:T(4,128)} %param.33) | copy-start | bytes 6148
  17.3 11.8 %copy-start.30 = (s32[15]{0:T(128)S(1)}, s32[15]{0:T(128)}, u32[]{:S(2)}) copy-start(s32[15]{0:T(128)} %constant.67.clone) | copy-start | bytes 184
  17.3 11.8 %copy-start.31 = (s32[15]{0:T(128)S(1)}, s32[15]{0:T(128)}, u32[]{:S(2)}) copy-start(s32[15]{0:T(128)} %constant.66.clone) | copy-start | bytes 184
  17.3 11.8 %copy-start.32 = (s32[15]{0:T(128)S(1)}, s32[15]{0:T(128)}, u32[]{:S(2)}) copy-start(s32[15]{0:T(128)} %constant.65.clone) | copy-start | bytes 184
  17.3 11.8 %copy-start.33 = (s32[15]{0:T(128)S(1)}, s32[15]{0:T(128)}, u32[]{:S(2)}) copy-start(s32[15]{0:T(128)} %constant.64.clone) | copy-start | bytes 184
  17.3 11.8 %copy-start.34 = (s32[15]{0:T(128)S(1)}, s32[15]{0:T(128)}, u32[]{:S(2)}) copy-start(s32[15]{0:T(128)} %constant.63.clone) | copy-start | bytes 184
  17.4 12.0 %copy-start.28 = (f32[4,128]{1,0:T(4,128)S(1)}, f32[4,128]{1,0:T(4,128)}, u32[]{:S(2)}) copy-start(f32[4,128]{1,0:T(4,128)} %param.32) | copy-start | bytes 6148
  17.4 12.0 %copy-start.1 = (f32[1,13,35,128]{3,0,2,1:T(1,128)S(1)}, f32[1,13,35,128]{3,0,2,1:T(1,128)}, u32[]{:S(2)}) copy-start(f32[1,13,35,128]{3,0,2,1:T(1,128)} %param.26) | copy-start | bytes 698884
  17.4 12.0 %copy-start.10 = (f32[3,35,35,1]{2,1,3,0:T(8,128)S(1)}, f32[3,35,35,1]{2,1,3,0:T(8,128)}, u32[]{:S(2)}) copy-start(f32[3,35,35,1]{2,1,3,0:T(8,128)} %constant.74) | copy-start | bytes 44104
  19.8 10.5 %copy-start.25 = (f32[3,3,128]{2,1,0:T(4,128)S(1)}, f32[3,3,128]{2,1,0:T(4,128)}, u32[]{:S(2)}) copy-start(f32[3,3,128]{2,1,0:T(4,128)} %param.30) | copy-start | bytes 13828
  19.8 10.5 %copy-start = (f32[6,35,128]{2,1,0:T(8,128)S(1)}, f32[6,35,128]{2,1,0:T(8,128)}, u32[]{:S(2)}) copy-start(f32[6,35,128]{2,1,0:T(8,128)} %param.28) | copy-start | bytes 322564
  19.8 10.5 %copy-start.16 = (f32[1,2,13,35,128]{4,1,3,2,0:T(2,128)S(1)}, f32[1,2,13,35,128]{4,1,3,2,0:T(2,128)}, u32[]{:S(2)}) copy-start(f32[1,2,13,35,128]{4,1,3,2,0:T(2,128)} %param.27) | copy-start | bytes 1397764
  19.8 19.8 %collective-permute-start.1 = (f32[13,15,64]{1,0,2:T(8,128)}, f32[13,15,64]{1,0,2:T(8,128)}, u32[]{:S(2)}, u32[]{:S(2)}) collective-permute-start(f32[13,15,64]{1,0,2:T(8,128)} %get-tuple-element.23), channel_id=1, source_target_pairs={{1,0},{2,1},{3,2},{4,3},{5,4},{6,5},{7,6},{9,8},{10,9},{11,10},{12... | collective-permute-start | bytes 149768 | tf_op jit(solution)/shard_map/ppermute | solution.py:20
  21.2 27.2 %collective-permute-start = (f32[13,15,64]{1,0,2:T(8,128)}, f32[13,15,64]{1,0,2:T(8,128)}, u32[]{:S(2)}, u32[]{:S(2)}) collective-permute-start(f32[13,15,64]{1,0,2:T(8,128)} %get-tuple-element.22), channel_id=1, source_target_pairs={{0,1},{1,2},{2,3},{3,4},{4,5},{5,6},{6,7},{8,9},{9,10},{10,11},{11... | collective-permute-start | bytes 149768 | tf_op jit(solution)/shard_map/ppermute | solution.py:19
  39.6 33.6 %copy-start.21 = (f32[3,4,128]{2,0,1:T(4,128)}, f32[3,4,128]{2,0,1:T(4,128)S(1)}, u32[]{:S(2)}) copy-start(f32[3,4,128]{2,0,1:T(4,128)S(1)} %copy.154) | copy-start | bytes 18436
  90.9 16.6 %collective-permute-start.3 = (f32[13,15,64]{1,0,2:T(8,128)S(1)}, f32[13,15,64]{1,0,2:T(8,128)}, u32[]{:S(2)}, u32[]{:S(2)}) collective-permute-start(f32[13,15,64]{1,0,2:T(8,128)S(1)} %get-tuple-element.21), channel_id=1, source_target_pairs={{1,0},{2,1},{3,2},{4,3},{5,4},{6,5},{7,6},{9,8},{10,9},{11,10},{12... | collective-permute-start | bytes 149768 | tf_op jit(solution)/shard_map/ppermute | solution.py:20
  92.2 26.7 %collective-permute-start.2 = (f32[13,15,64]{1,0,2:T(8,128)}, f32[13,15,64]{1,0,2:T(8,128)}, u32[]{:S(2)}, u32[]{:S(2)}) collective-permute-start(f32[13,15,64]{1,0,2:T(8,128)} %get-tuple-element.20), channel_id=1, source_target_pairs={{0,1},{1,2},{2,3},{3,4},{4,5},{5,6},{6,7},{8,9},{9,10},{10,11},{11... | collective-permute-start | bytes 149768 | tf_op jit(solution)/shard_map/ppermute | solution.py:19
  146.5 81.4 %copy-start.4 = (f32[1,6,35,128]{3,2,1,0:T(8,128)S(1)}, f32[1,6,35,128]{3,2,1,0:T(8,128)}, u32[]{:S(2)}) copy-start(f32[1,6,35,128]{3,2,1,0:T(8,128)} %get-tuple-element.39) | copy-start | bytes 322564
  146.6 104.0 %copy-start.5 = (f32[1,6,35,128]{3,2,1,0:T(8,128)S(1)}, f32[1,6,35,128]{3,2,1,0:T(8,128)}, u32[]{:S(2)}) copy-start(f32[1,6,35,128]{3,2,1,0:T(8,128)} %get-tuple-element.72) | copy-start | bytes 322564
  146.6 123.8 %copy-start.7 = (f32[1,6,35,128]{3,2,1,0:T(8,128)S(1)}, f32[1,6,35,128]{3,2,1,0:T(8,128)}, u32[]{:S(2)}) copy-start(f32[1,6,35,128]{3,2,1,0:T(8,128)} %get-tuple-element.37) | copy-start | bytes 322564
  (17 other events, 68.5 us)
Sparse Core Ops, SparseCore 0:
  150.0 31.6 all-reduce.2
where the time goes:
time: 406 us; the launch traced here: 405 us
  blocking collectives  190 us (47%)
  local copies, waits for them, and re-layouts  81.3 us (20%)
  waiting for transfers between devices  53.4 us (13%)
  between operations  29.4 us (7%)
  matrix products  19.9 us (5%)
  other arithmetic  16.3 us (4%)
  starting transfers between devices  14.9 us (4%)
    psum x10, blocking collectives, combine_sums(): return lax.psum(values, 'mesh')  190 us
    gather x2, local copies, waits for them, and re-layouts, shards(): turned = ghosts.reshape(fields, face_width * slot_count)[:, flat_index]  34.6 us
    psum x1, waiting for transfers between devices, shards(): total_grad = lax.psum(gradient, 'shot')  31.2 us
    ppermute x2, waiting for transfers between devices, padded(): before = lax.ppermute(last, axis, up)  17.7 us
    ppermute x2, starting transfers between devices, padded(): before = lax.ppermute(last, axis, up)  12.1 us
    reshape x4, local copies, waits for them, and re-layouts, shards(): flat_trace = inner_trace.reshape(fields, face_width, 4 * elements)  8.56 us
  transfers between devices with their start and end apart: 5, of which 4 were waited for; matrix products, arithmetic and copies ran while one was open for 5% of the time, Pallas kernels for 0%

commit v1 on v0

--- a/solution.py
+++ b/solution.py
@@ -7,6 +7,17 @@
 
 HIGH = lax.Precision.HIGHEST
 STEP_SIZE = 0.02
+
+
+def follow_the_leaf(w_in, chip_axis):
+    ready = w_in
+    lanes = jax.lax.axis_size(chip_axis)
+    for num in [ix for ix in (1, 2, 4, 8, 16) if ix < lanes]:
+        nodes = []
+        for dev_i in range(lanes):
+            nodes.append((dev_i, dev_i ^ num))
+        ready = ready + jax.lax.ppermute(ready, chip_axis, nodes)
+    return ready
 
 
 def padded(x, sides, width):
@@ -222,7 +233,7 @@
         gradient = gradient + STEP_SIZE * kernel_term(
             adjoint, forward_states[0, step_index], coupling, metric, derivs
         )
-    total_grad = lax.psum(gradient, "shot")
+    total_grad = follow_the_leaf(gradient, "shot")
 
     def combine_sums(values):
         return lax.psum(values, "mesh")

time: 406 us -> 363 us (0.89)
  waiting for transfers between devices: 53.4 us -> 26.4 us
  between operations: 29.4 us -> 15.9 us
    psum x1 -> x0, waiting for transfers between devices: 31.2 us -> none  [shards(): total_grad = lax.psum(gradient, 'shot')]
    ppermute x0 -> x2, waiting for transfers between devices: none -> 4.28 us  [follow_the_leaf(): ready = ready + jax.lax.ppermute(ready, chip_axis, nodes)]
  transfers between devices with their start and end apart: 5 -> 6, of which waited for: 4 -> 5; matrix products, arithmetic and copies ran while one was open for 5% -> 6% of each run, Pallas kernels for 0% -> 0%
where the time goes in v1:
time: 363 us; the launch traced here: 362 us
  blocking collectives  189 us (52%)
  local copies, waits for them, and re-layouts  82 us (23%)
  waiting for transfers between devices  26.4 us (7%)
  matrix products  19.9 us (5%)
  starting transfers between devices  16.5 us (5%)
  between operations  15.9 us (4%)
  other arithmetic  13.1 us (4%)
    psum x10, blocking collectives, combine_sums(): return lax.psum(values, 'mesh')  189 us
    gather x2, local copies, waits for them, and re-layouts, shards(): turned = ghosts.reshape(fields, face_width * slot_count)[:, flat_index]  34.6 us
    ppermute x2, waiting for transfers between devices, padded(): before = lax.ppermute(last, axis, up)  17.6 us
    ppermute x2, starting transfers between devices, padded(): before = lax.ppermute(last, axis, up)  12.2 us
    reshape x4, local copies, waits for them, and re-layouts, shards(): flat_trace = inner_trace.reshape(fields, face_width, 4 * elements)  8.56 us
    gather x2, local copies, waits for them, and re-layouts, shards(): sent_traces = flat_trace[:, :, send_faces]  7.74 us
  transfers between devices with their start and end apart: 6, of which 5 were waited for; matrix products, arithmetic and copies ran while one was open for 6% of the time, Pallas kernels for 0%

profile of v1, /device:TPU:0, one launch (start us, length us, event | category | flops | bytes accessed | tf_op | source)
XLA Modules:
  0.0 362.4 jit_solution(15135836400248404411)
XLA Ops:
  3.3 3.6 copy.157
  6.9 3.8 %gather_fusion.2 = f32[128,13,15]{2,1,0:T(8,128)} fusion(f32[13,15,512]{1,0,2:T(8,128)} %copy.157, s32[1024]{0:T(1024)S(1)} %pad_clamp_fusion.1), kind=kCustom, calls=%fused_computation.2 | custom fusion | bytes 200192 | tf_op jit(solution)/shard_map/gather | solution.py:222
  14.6 6.3 %collective-permute-start = (f32[13,15,64]{1,0,2:T(8,128)}, f32[13,15,64]{1,0,2:T(8,128)}, u32[]{:S(2)}, u32[]{:S(2)}) collective-permute-start(f32[13,15,64]{1,0,2:T(8,128)} %get-tuple-element.24), channel_id=1, source_target_pairs={{0,1},{1,2},{2,3},{3,4},{4,5},{5,6},{6,7},{8,9},{9,10},{10,11},{11... | collective-permute-start | bytes 149768 | tf_op jit(solution)/shard_map/ppermute | solution.py:30
  34.3 7.5 %collective-permute-done = f32[13,15,64]{1,0,2:T(8,128)} collective-permute-done((f32[13,15,64]{1,0,2:T(8,128)}, f32[13,15,64]{1,0,2:T(8,128)}, u32[]{:S(2)}, u32[]{:S(2)}) %collective-permute-start) | collective-permute-done | bytes 49952 | tf_op jit(solution)/shard_map/ppermute | solution.py:30
  46.4 17.3 %gather_fusion.3 = f32[7680,13]{1,0:T(8,128)} fusion(f32[13,9600]{0,1:T(8,128)} %bitcast.349, s32[8192]{0:T(1024)S(1)} %pad_clamp_fusion), kind=kCustom, calls=%fused_computation.3 | custom fusion | bytes 829440 | tf_op jit(solution)/shard_map/gather | solution.py:227
  66.6 3.6 %fusion.1 = f32[13,15,4,128]{3,0,2,1:T(8,128)S(1)} fusion(f32[6,15,4,128]{3,0,2,1:T(8,128)} %bitcast.361, f32[13,15,4,128]{3,0,2,1:T(8,128)S(1)} %sub.44, f32[3,4,128]{2,0,1:T(4,128)S(1)} %copy.154, f32[3,6,13,13]{3,2,1,0:T(8,128)S(1)} %copy-done.13), kind=kOutput, calls=%fused_computation.10 | convolution fusion | flops 281748480 | bytes 1001352 | tf_op jit(solution)/shard_map/dpfg,dfnxe->pgnxe/dot_general | solution.py:154
  74.6 3.6 copy.170
  78.2 3.9 %gather_fusion.5 = f32[128,13,15]{2,1,0:T(8,128)} fusion(f32[13,15,512]{1,0,2:T(8,128)} %copy.170, s32[1024]{0:T(1024)} %copy-done.24), kind=kCustom, calls=%fused_computation.5 | custom fusion | bytes 200192 | tf_op jit(solution)/shard_map/gather | solution.py:222
  85.6 5.8 %collective-permute-start.2 = (f32[13,15,64]{1,0,2:T(8,128)}, f32[13,15,64]{1,0,2:T(8,128)}, u32[]{:S(2)}, u32[]{:S(2)}) collective-permute-start(f32[13,15,64]{1,0,2:T(8,128)} %get-tuple-element.22), channel_id=1, source_target_pairs={{0,1},{1,2},{2,3},{3,4},{4,5},{5,6},{6,7},{8,9},{9,10},{10,11},{11... | collective-permute-start | bytes 149768 | tf_op jit(solution)/shard_map/ppermute | solution.py:30
  96.4 4.5 %collective-permute-done.3 = f32[13,15,64]{1,0,2:T(8,128)} collective-permute-done((f32[13,15,64]{1,0,2:T(8,128)S(1)}, f32[13,15,64]{1,0,2:T(8,128)}, u32[]{:S(2)}, u32[]{:S(2)}) %collective-permute-start.3) | collective-permute-done | bytes 49952 | tf_op jit(solution)/shard_map/ppermute | solution.py:31
  102.2 10.1 %collective-permute-done.2 = f32[13,15,64]{1,0,2:T(8,128)} collective-permute-done((f32[13,15,64]{1,0,2:T(8,128)}, f32[13,15,64]{1,0,2:T(8,128)}, u32[]{:S(2)}, u32[]{:S(2)}) %collective-permute-start.2) | collective-permute-done | bytes 49952 | tf_op jit(solution)/shard_map/ppermute | solution.py:30
  113.7 3.2 copy.173
  116.9 17.3 %gather_fusion.6 = f32[7680,13]{1,0:T(8,128)} fusion(f32[13,9600]{0,1:T(8,128)} %bitcast.348, s32[8192]{0:T(1024)S(1)} %pad_clamp_fusion), kind=kCustom, calls=%fused_computation.6 | custom fusion | bytes 829440 | tf_op jit(solution)/shard_map/gather | solution.py:227
  146.4 3.6 collective-permute-done.5
  150.6 20.9 %all-reduce = (f32[]{:T(128)}, f32[6]{0:T(128)S(1)}) all-reduce(f32[]{:T(128)} %get-tuple-element.20, f32[6]{0:T(128)S(1)} %pad_maximum_fusion.2), channel_id=1, replica_groups=mesh['shot'=4,'mesh'=8] {'mesh'}, use_global_device_ids=true, to_apply=%region_10.0 | all-reduce | flops 7 | bytes 56 | tf_op jit(solution)/shard_map/psum | solution.py:239
  174.2 17.8 %psum.79 = f32[]{:T(128)} all-reduce(f32[]{:T(128)} %fusion.63), channel_id=1, replica_groups=mesh['shot'=4,'mesh'=8] {'mesh'}, use_global_device_ids=true, to_apply=%region_12.0 | all-reduce | flops 1 | bytes 8 | tf_op jit(solution)/shard_map/psum | solution.py:239
  193.9 19.7 %psum.80 = f32[]{:T(128)} all-reduce(f32[]{:T(128)} %get-tuple-element.18), channel_id=1, replica_groups=mesh['shot'=4,'mesh'=8] {'mesh'}, use_global_device_ids=true, to_apply=%region_14.0 | all-reduce | flops 1 | bytes 8 | tf_op jit(solution)/shard_map/psum | solution.py:239
  215.7 17.8 %psum.81 = f32[]{:T(128)} all-reduce(f32[]{:T(128)} %fusion.47), channel_id=1, replica_groups=mesh['shot'=4,'mesh'=8] {'mesh'}, use_global_device_ids=true, to_apply=%region_16.0 | all-reduce | flops 1 | bytes 8 | tf_op jit(solution)/shard_map/psum | solution.py:239
  235.4 19.7 %psum.82 = f32[]{:T(128)} all-reduce(f32[]{:T(128)} %get-tuple-element.16), channel_id=1, replica_groups=mesh['shot'=4,'mesh'=8] {'mesh'}, use_global_device_ids=true, to_apply=%region_18.0 | all-reduce | flops 1 | bytes 8 | tf_op jit(solution)/shard_map/psum | solution.py:239
  258.4 17.8 %psum.83 = f32[]{:T(128)} all-reduce(f32[]{:T(128)} %fusion.36), channel_id=1, replica_groups=mesh['shot'=4,'mesh'=8] {'mesh'}, use_global_device_ids=true, to_apply=%region_20.0 | all-reduce | flops 1 | bytes 8 | tf_op jit(solution)/shard_map/psum | solution.py:239
  278.2 19.7 %psum.84 = f32[]{:T(128)} all-reduce(f32[]{:T(128)} %fusion.44), channel_id=1, replica_groups=mesh['shot'=4,'mesh'=8] {'mesh'}, use_global_device_ids=true, to_apply=%region_22.0 | all-reduce | flops 1 | bytes 8 | tf_op jit(solution)/shard_map/psum | solution.py:239
  299.9 17.8 %psum.85 = f32[]{:T(128)} all-reduce(f32[]{:T(128)} %get-tuple-element.14), channel_id=1, replica_groups=mesh['shot'=4,'mesh'=8] {'mesh'}, use_global_device_ids=true, to_apply=%region_24.0 | all-reduce | flops 1 | bytes 8 | tf_op jit(solution)/shard_map/psum | solution.py:239
  320.6 19.7 %psum.86 = f32[]{:T(128)} all-reduce(f32[]{:T(128)} %fusion.60), channel_id=1, replica_groups=mesh['shot'=4,'mesh'=8] {'mesh'}, use_global_device_ids=true, to_apply=%region_26.0 | all-reduce | flops 1 | bytes 8 | tf_op jit(solution)/shard_map/psum | solution.py:239
  342.3 17.8 %psum.87 = f32[]{:T(128)} all-reduce(f32[]{:T(128)} %get-tuple-element.12), channel_id=1, replica_groups=mesh['shot'=4,'mesh'=8] {'mesh'}, use_global_device_ids=true, to_apply=%region_28.0 | all-reduce | flops 1 | bytes 8 | tf_op jit(solution)/shard_map/psum | solution.py:239
  (159 shorter events, 63.5 us)
Async XLA Ops:
  3.2 17.7 %copy-start.2 = (f32[5,6,35,128]{3,2,1,0:T(8,128)S(1)}, f32[5,6,35,128]{3,2,1,0:T(8,128)}, u32[]{:S(2)}) copy-start(f32[5,6,35,128]{3,2,1,0:T(8,128)} %param.37) | copy-start | bytes 1612804
  3.3 17.7 %copy-start.3 = (f32[5,6,35,128]{3,2,1,0:T(8,128)S(1)}, f32[5,6,35,128]{3,2,1,0:T(8,128)}, u32[]{:S(2)}) copy-start(f32[5,6,35,128]{3,2,1,0:T(8,128)} %param.36) | copy-start | bytes 1612804
  6.9 15.6 %copy-start.27 = (s32[4,128]{1,0:T(4,128)S(1)}, s32[4,128]{1,0:T(4,128)}, u32[]{:S(2)}) copy-start(s32[4,128]{1,0:T(4,128)} %param.34) | copy-start | bytes 6148
  10.7 11.8 %copy-start.28 = (s32[4,128]{1,0:T(4,128)S(1)}, s32[4,128]{1,0:T(4,128)}, u32[]{:S(2)}) copy-start(s32[4,128]{1,0:T(4,128)} %param.33) | copy-start | bytes 6148
  10.7 11.8 %copy-start.31 = (s32[15]{0:T(128)S(1)}, s32[15]{0:T(128)}, u32[]{:S(2)}) copy-start(s32[15]{0:T(128)} %constant.67.clone) | copy-start | bytes 184
  10.7 11.8 %copy-start.32 = (s32[15]{0:T(128)S(1)}, s32[15]{0:T(128)}, u32[]{:S(2)}) copy-start(s32[15]{0:T(128)} %constant.66.clone) | copy-start | bytes 184
  10.7 11.8 %copy-start.33 = (s32[15]{0:T(128)S(1)}, s32[15]{0:T(128)}, u32[]{:S(2)}) copy-start(s32[15]{0:T(128)} %constant.65.clone) | copy-start | bytes 184
  10.8 11.8 %copy-start.34 = (s32[15]{0:T(128)S(1)}, s32[15]{0:T(128)}, u32[]{:S(2)}) copy-start(s32[15]{0:T(128)} %constant.64.clone) | copy-start | bytes 184
  10.8 11.8 %copy-start.35 = (s32[15]{0:T(128)S(1)}, s32[15]{0:T(128)}, u32[]{:S(2)}) copy-start(s32[15]{0:T(128)} %constant.63.clone) | copy-start | bytes 184
  10.8 12.0 %copy-start.29 = (f32[4,128]{1,0:T(4,128)S(1)}, f32[4,128]{1,0:T(4,128)}, u32[]{:S(2)}) copy-start(f32[4,128]{1,0:T(4,128)} %param.32) | copy-start | bytes 6148
  10.8 12.0 %copy-start.1 = (f32[1,13,35,128]{3,0,2,1:T(1,128)S(1)}, f32[1,13,35,128]{3,0,2,1:T(1,128)}, u32[]{:S(2)}) copy-start(f32[1,13,35,128]{3,0,2,1:T(1,128)} %param.26) | copy-start | bytes 698884
  10.8 12.0 %copy-start.10 = (f32[3,35,35,1]{2,1,3,0:T(8,128)S(1)}, f32[3,35,35,1]{2,1,3,0:T(8,128)}, u32[]{:S(2)}) copy-start(f32[3,35,35,1]{2,1,3,0:T(8,128)} %constant.74) | copy-start | bytes 44104
  13.2 19.8 %collective-permute-start.1 = (f32[13,15,64]{1,0,2:T(8,128)}, f32[13,15,64]{1,0,2:T(8,128)}, u32[]{:S(2)}, u32[]{:S(2)}) collective-permute-start(f32[13,15,64]{1,0,2:T(8,128)} %get-tuple-element.25), channel_id=1, source_target_pairs={{1,0},{2,1},{3,2},{4,3},{5,4},{6,5},{7,6},{9,8},{10,9},{11,10},{12... | collective-permute-start | bytes 149768 | tf_op jit(solution)/shard_map/ppermute | solution.py:31
  14.6 27.2 %collective-permute-start = (f32[13,15,64]{1,0,2:T(8,128)}, f32[13,15,64]{1,0,2:T(8,128)}, u32[]{:S(2)}, u32[]{:S(2)}) collective-permute-start(f32[13,15,64]{1,0,2:T(8,128)} %get-tuple-element.24), channel_id=1, source_target_pairs={{0,1},{1,2},{2,3},{3,4},{4,5},{5,6},{6,7},{8,9},{9,10},{10,11},{11... | collective-permute-start | bytes 149768 | tf_op jit(solution)/shard_map/ppermute | solution.py:30
  32.4 34.2 %copy-start.22 = (f32[3,4,128]{2,0,1:T(4,128)}, f32[3,4,128]{2,0,1:T(4,128)S(1)}, u32[]{:S(2)}) copy-start(f32[3,4,128]{2,0,1:T(4,128)S(1)} %copy.154) | copy-start | bytes 18436
  84.3 16.6 %collective-permute-start.3 = (f32[13,15,64]{1,0,2:T(8,128)S(1)}, f32[13,15,64]{1,0,2:T(8,128)}, u32[]{:S(2)}, u32[]{:S(2)}) collective-permute-start(f32[13,15,64]{1,0,2:T(8,128)S(1)} %get-tuple-element.23), channel_id=1, source_target_pairs={{1,0},{2,1},{3,2},{4,3},{5,4},{6,5},{7,6},{9,8},{10,9},{11,10},{12... | collective-permute-start | bytes 149768 | tf_op jit(solution)/shard_map/ppermute | solution.py:31
  85.6 26.7 %collective-permute-start.2 = (f32[13,15,64]{1,0,2:T(8,128)}, f32[13,15,64]{1,0,2:T(8,128)}, u32[]{:S(2)}, u32[]{:S(2)}) collective-permute-start(f32[13,15,64]{1,0,2:T(8,128)} %get-tuple-element.22), channel_id=1, source_target_pairs={{0,1},{1,2},{2,3},{3,4},{4,5},{5,6},{6,7},{8,9},{9,10},{10,11},{11... | collective-permute-start | bytes 149768 | tf_op jit(solution)/shard_map/ppermute | solution.py:30
  140.0 33.5 %copy-start.4 = (f32[1,6,35,128]{3,2,1,0:T(8,128)S(1)}, f32[1,6,35,128]{3,2,1,0:T(8,128)}, u32[]{:S(2)}) copy-start(f32[1,6,35,128]{3,2,1,0:T(8,128)} %get-tuple-element.72) | copy-start | bytes 322564
  140.0 53.3 %copy-start.5 = (f32[1,6,35,128]{3,2,1,0:T(8,128)S(1)}, f32[1,6,35,128]{3,2,1,0:T(8,128)}, u32[]{:S(2)}) copy-start(f32[1,6,35,128]{3,2,1,0:T(8,128)} %get-tuple-element.41) | copy-start | bytes 322564
  140.0 75.0 %copy-start.6 = (f32[1,6,35,128]{3,2,1,0:T(8,128)S(1)}, f32[1,6,35,128]{3,2,1,0:T(8,128)}, u32[]{:S(2)}) copy-start(f32[1,6,35,128]{3,2,1,0:T(8,128)} %get-tuple-element.74) | copy-start | bytes 322564
  140.7 93.9 %copy-start.7 = (f32[1,6,35,128]{3,2,1,0:T(8,128)S(1)}, f32[1,6,35,128]{3,2,1,0:T(8,128)}, u32[]{:S(2)}) copy-start(f32[1,6,35,128]{3,2,1,0:T(8,128)} %get-tuple-element.39) | copy-start | bytes 322564
  142.6 1.4 collective-permute-start.4
  144.1 217.3 %copy-start.16 = (f32[1,6,35,128]{3,1,2,0:T(8,128)S(1)}, f32[1,6,35,128]{3,1,2,0:T(8,128)}, u32[]{:S(2)}) copy-start(f32[1,6,35,128]{3,1,2,0:T(8,128)} %copy.411) | copy-start | bytes 322564
  144.1 5.9 %collective-permute-start.5 = (f32[6,35,128]{2,0,1:T(8,128)S(1)}, f32[6,35,128]{2,0,1:T(8,128)S(1)}, u32[]{:S(2)}, u32[]{:S(2)}) collective-permute-start(f32[6,35,128]{2,0,1:T(8,128)S(1)} %add.309), channel_id=1, source_target_pairs={{0,16},{8,24},{16,0},{24,8},{1,17},{9,25},{17,1},{25,9},{2,18},{10... | collective-permute-start | bytes 322568 | tf_op jit(solution)/shard_map/ppermute | solution.py:19
  (19 other events, 97.7 us)
